TPU v7x, 128 devices: a whole 4x4x4 slice. The times are simulated.
128 devices in a mesh: prow: 16 (over y, x_hi, core), pcol: 8 (over x_lo, z).
Axes of the slice: x: 4 (x_hi: 2, x_lo: 2; x = x_hi * 2 + x_lo), y: 4, z: 4, core: 2. Of those that a mesh axis runs over, the one named last changes fastest.
Arguments:
- inverse_block: float32 [3, 16, 256, 6, 8, 256], P(None, 'prow', None, None, 'pcol'), as said below
- panel_first: float32 [3, 16, 256, 512], P(None, 'prow', 'pcol'), may hold values from -0.0546875 to 0.0546875
- panel_second: float32 [3, 16, 256, 512], P(None, 'prow', 'pcol'), may hold values from -0.0546875 to 0.0546875
- diag_first: float32 [512, 512], replicated, may hold values from -6 to 6
- diag_second: float32 [512, 512], replicated, may hold values from -6 to 6
- pattern_first: int32 [48], replicated, may hold values from 0 to 1, as said below
- pattern_second: int32 [48], replicated, may hold values from 0 to 1, as said below
Outputs:
- column_first: float32 [3, 16, 256, 512], P(None, 'prow', 'pcol')
- column_second: float32 [3, 16, 256, 512], P(None, 'prow', 'pcol')
- diagonal_first: float32 [512, 512], replicated
- diagonal_second: float32 [512, 512], replicated
Inputs may be any that keep to these rules, and one draw needn't show every extreme that they name: inverse_block is symmetric as a matrix of 12288 rows: its entry (i, j) equals its entry (j, i) exactly. `pattern_first`: at least one entry is 1. `pattern_second`: at least one entry is 1.
All inputs are finite; a program needn't handle non-finite values.
Results may differ from a plain program's by a relative error of at most 0.000071.
Values sent between devices are 32-bit elements; how exact they have to be, the bound alone decides.
No kernel may reach another device: no remote copies, remote signals or barrier semaphores. Data moves between devices by JAX's collectives and lax.ppermute only.
A program may use at most 64 MiB of HBM per device.

v0:
```python
import jax
import jax.numpy as jnp
from jax import lax
from jax.sharding import PartitionSpec as P


TILE = 128
PIECE = 512


def pack_upper(d):
    n = d.shape[-1] // TILE
    blocks = [
        d[..., i * TILE:(i + 1) * TILE, j * TILE:(j + 1) * TILE]
        for i in range(n)
        for j in range(i, n)
    ]
    return jnp.stack(blocks, axis=-3)


def unpack_upper(packed, n):
    rows = [[None] * n for _ in range(n)]
    k = 0
    for i in range(n):
        for j in range(i, n):
            blk = packed[..., k, :, :]
            rows[i][j] = blk
            if i != j:
                rows[j][i] = jnp.swapaxes(blk, -1, -2)
            k += 1
    return jnp.concatenate([jnp.concatenate(r, axis=-1) for r in rows], axis=-2)


def body(
    inverse_block, panel_first, panel_second, diag_first, diag_second, pattern_first, pattern_second
):
    prow = ("prow_hi", "core")
    row_count = lax.axis_size(prow)
    pair = lax.axis_size("core")
    core = lax.axis_index("core")
    col_count = lax.axis_size("pcol")
    row_index = lax.axis_index(prow)
    col_index = lax.axis_index("pcol")
    row_blocks = inverse_block.shape[0]
    block_rows = inverse_block.shape[2]
    col_blocks = inverse_block.shape[3]
    slice_rows = panel_first.shape[2]
    width = panel_first.shape[3]
    highest = lax.Precision.HIGHEST
    both = ("prow_hi", "core", "pcol")
    swap = [(b, (b + 1) % pair) for b in range(pair)]

    def pair_sum(value, axis):
        split = value.reshape(value.shape[:axis] + (value.shape[axis] // pair, pair) + value.shape[axis + 1:])
        mine = lax.dynamic_index_in_dim(split, core, axis + 1, False)
        other = lax.dynamic_index_in_dim(split, (core + 1) % pair, axis + 1, False)
        return mine + lax.ppermute(other, "core", swap)

    def kept_of(pattern, prow):
        return lax.dynamic_index_in_dim(
            pattern.reshape(row_blocks, row_count), prow, 1, False
        ).astype(jnp.float32)

    own_first = kept_of(pattern_first, row_index)
    own_second = kept_of(pattern_second, row_index)
    x = jnp.concatenate(
        [
            panel_first[:, 0] * own_first[:, None, None],
            panel_second[:, 0] * own_second[:, None, None],
        ],
        axis=-1,
    )

    to_reducer = []
    to_owner = []
    for q in range(row_count):
        for c in range(col_count):
            reducer = (col_count * (q // col_count) + c) * col_count + q % col_count
            to_reducer.append((q * col_count + c, reducer))
            to_owner.append((reducer, q * col_count + c))
    x_at_reducer = lax.ppermute(x, both, to_reducer)

    matrix = inverse_block.reshape(row_blocks, block_rows, col_blocks, block_rows)

    def reduce_inner(piece, by_permutes):
        gathered = gather_piece(piece, by_permutes)
        return reduce_gathered(piece, gathered)

    def gather_piece(piece, by_permutes):
        if by_permutes:
            held = [None] * col_count
            held[0] = piece
            for k in range(1, col_count):
                held[k] = lax.ppermute(
                    piece, "pcol", [(i, (i + k) % col_count) for i in range(col_count)]
                )
            order = jnp.stack(held, axis=1)
            source = (col_index - jnp.arange(col_count)) % col_count
            slot = jnp.argsort(source)
            gathered = jnp.take(order, slot, axis=1).reshape(row_blocks, block_rows, piece.shape[-1])
        else:
            spread = jnp.broadcast_to(
                piece[:, None], (row_blocks, col_count) + piece.shape[1:]
            ).reshape(row_blocks, block_rows, piece.shape[-1])
            gathered = lax.all_to_all(spread, "pcol", 1, 1, tiled=True)
        return gathered

    def reduce_gathered(piece, gathered):
        partial = jnp.einsum(
            "lsmt,lsw->mtw",
            matrix,
            gathered,
            precision=highest,
            preferred_element_type=jnp.float32,
        )
        chunks = partial.reshape(row_blocks, row_count, slice_rows, piece.shape[-1])
        received = lax.all_to_all(pair_sum(chunks, 1), "prow_hi", 1, 1, tiled=True)
        return jnp.sum(received, axis=1)

    total = jnp.concatenate(
        [reduce_inner(x[..., k * PIECE:(k + 1) * PIECE], k > 0) for k in range(2 * width // PIECE)],
        axis=-1,
    )

    owner_row = col_index + col_count * (row_index // col_count)
    kept_first = kept_of(pattern_first, owner_row)
    kept_second = kept_of(pattern_second, owner_row)
    column = jnp.concatenate(
        [
            -(total[..., :width] * kept_first[:, None, None]),
            -(total[..., width:] * kept_second[:, None, None]),
        ],
        axis=-1,
    )
    parts = jnp.stack(
        [
            jnp.einsum(
                "lsw,lsv->wv",
                x_at_reducer[..., :width],
                column[..., :width],
                precision=highest,
                preferred_element_type=jnp.float32,
            ),
            jnp.einsum(
                "lsw,lsv->wv",
                x_at_reducer[..., width:],
                column[..., width:],
                precision=highest,
                preferred_element_type=jnp.float32,
            ),
        ]
    )
    column_home = lax.ppermute(column, both, to_owner)
    packed = pack_upper(parts)
    others = ("prow_hi", "pcol")
    devices = lax.axis_size(others)
    half = pair_sum(packed.reshape(pair * devices, packed.size // (pair * devices)), 0)
    flat = half.reshape(devices, half.size // devices)
    reduced = jnp.sum(lax.all_to_all(flat, others, 0, 0, tiled=True), axis=0)
    spread_sum = jnp.broadcast_to(reduced[None], flat.shape)
    mine = lax.all_to_all(spread_sum, others, 0, 0, tiled=True).reshape(half.shape)
    other = lax.ppermute(mine, "core", swap)
    summed = jnp.where(
        core == 0,
        jnp.stack([mine, other], axis=1),
        jnp.stack([other, mine], axis=1),
    ).reshape(packed.shape)
    sums = unpack_upper(summed, width // TILE)
    return (
        column_home[:, None, :, :width],
        column_home[:, None, :, width:],
        diag_first - sums[0],
        diag_second - sums[1],
    )


def solution(mesh):
    rows, cols = mesh.devices.shape
    split = jax.sharding.Mesh(mesh.devices.reshape(rows // 2, 2, cols), ("prow_hi", "core", "pcol"))
    prow = ("prow_hi", "core")
    placed = (
        P(None, prow, None, None, "pcol", None),
        P(None, prow, "pcol", None),
        P(None, prow, "pcol", None),
        P(),
        P(),
        P(),
        P(),
    )

    return jax.shard_map(
        body,
        mesh=split,
        in_specs=placed,
        out_specs=(P(None, prow, "pcol", None), P(None, prow, "pcol", None), P(), P()),
        check_vma=False,
    )
```

profile of v0, /device:TPU:6, one launch (start us, length us, event | category | flops | bytes accessed | tf_op | source)
XLA Modules:
  0.0 243.2 jit_solution(8881438911809171003)
XLA Ops:
  3.4 2.0 collective-permute-start.1
  5.4 3.6 %collective-permute-start.2 = (f32[3,32,512]{2,1,0:T(8,128)S(1)}, f32[3,32,512]{2,1,0:T(8,128)S(1)}, u32[]{:S(2)}, u32[]{:S(2)}) collective-permute-start(f32[3,32,512]{2,1,0:T(8,128)S(1)} %bitcast_multiply_fusion.1), channel_id=1, source_target_pairs={{0,2},{1,3},{2,4},{3,5},{4,6},{5,7},{6,0},{7,1},{8,10},{9,11},{10,... | collective-permute-start | bytes 589832 | tf_op jit(solution)/shard_map/ppermute | solution.py:94
  15.5 4.9 %all-to-all-start = ((f32[3,256,512]{2,0,1:T(4,128)}), f32[3,256,512]{2,0,1:T(4,128)S(1)}, u32[]{:S(2)}, u32[]{:S(2)}) async-start(f32[3,256,512]{2,0,1:T(4,128)} %bitcast.1), calls=%async_computation | async-start | bytes 4194304 | tf_op jit(solution)/shard_map/all_to_all | solution.py:105
  22.2 3.0 %collective-permute-start.6 = (f32[3,32,512]{2,1,0:T(8,128)S(1)}, f32[3,32,512]{2,1,0:T(8,128)S(1)}, u32[]{:S(2)}, u32[]{:S(2)}) collective-permute-start(f32[3,32,512]{2,1,0:T(8,128)S(1)} %bitcast_multiply_fusion.1), channel_id=1, source_target_pairs={{0,6},{1,7},{2,0},{3,1},{4,2},{5,3},{6,4},{7,5},{8,14},{9,15},{10,... | collective-permute-start | bytes 589832 | tf_op jit(solution)/shard_map/ppermute | solution.py:94
  29.9 23.6 %collective-permute-done.6 = f32[3,32,512]{2,1,0:T(8,128)S(1)} collective-permute-done((f32[3,32,512]{2,1,0:T(8,128)S(1)}, f32[3,32,512]{2,1,0:T(8,128)S(1)}, u32[]{:S(2)}, u32[]{:S(2)}) %collective-permute-start.6) | collective-permute-done | bytes 196640 | tf_op jit(solution)/shard_map/ppermute | solution.py:94
  54.9 3.2 %gather_fusion = f32[8,3,32,512]{3,2,1,0:T(8,128)} fusion(f32[3,8,32,512]{3,2,0,1:T(8,128)} %bitcast_dynamic-update-slice_fusion, s32[1024]{0:T(1024)S(1)} %pad_clamp_fusion), kind=kCustom, calls=%fused_computation | custom fusion | bytes 3145760 | tf_op jit(solution)/shard_map/jit(_take)/gather | solution.py:100
  59.9 9.8 %fusion = f32[512,6,256,1]{0,2,3,1:T(8,128)S(1)} fusion(f32[3,256,512,1]{2,1,0,3:T(8,128)S(1)} %bitcast.186, f32[3,1,256,6,1,256]{5,4,3,2,1,0:T(1,128)} %param.7), kind=kOutput, calls=%fused_computation.1 | convolution fusion | flops 7247757312 | bytes 9437184 | tf_op jit(solution)/shard_map/lsmt,lsw->mtw/dot_general | solution.py:109
  72.5 10.4 %fusion.2 = f32[512,6,256,1]{0,2,3,1:T(8,128)S(1)} fusion(f32[3,1,256,6,1,256]{5,4,3,2,1,0:T(1,128)} %param.7, f32[3,256,512]{2,0,1:T(4,128)S(1)} %all-to-all-done), kind=kOutput, calls=%fused_computation.3 | convolution fusion | flops 7247757312 | bytes 9437184 | tf_op jit(solution)/shard_map/lsmt,lsw->mtw/dot_general | solution.py:109
  85.2 2.9 %bitcast_add_fusion = f32[3,8,32,512]{3,2,0,1:T(8,128)} fusion(f32[3,8,32,512]{3,2,0,1:T(8,128)} %collective-permute-done.8, f32[3,8,1,32,512]{4,3,2,1,0:T(8,128)S(1)} %copy-done), kind=kLoop, calls=%fused_computation.8 | loop fusion | flops 393216 | bytes 4718592 | tf_op jit(solution)/shard_map/add | solution.py:57
  88.2 7.4 %all-to-all-start.2 = ((f32[3,8,32,512]{3,2,0,1:T(8,128)}), f32[3,8,32,512]{3,2,0,1:T(8,128)S(1)}, u32[]{:S(2)}, u32[]{:S(2)}) async-start(f32[3,8,32,512]{3,2,0,1:T(8,128)} %bitcast_add_fusion), calls=%async_computation.2 | async-start | bytes 3145728 | tf_op jit(solution)/shard_map/all_to_all | solution.py:117
  95.6 2.9 %bitcast_add_fusion.1 = f32[3,8,32,512]{3,2,0,1:T(8,128)} fusion(f32[3,8,32,512]{3,2,0,1:T(8,128)} %collective-permute-done, f32[3,8,1,32,512]{4,3,2,1,0:T(8,128)S(1)} %get-tuple-element.10), kind=kLoop, calls=%fused_computation.9 | loop fusion | flops 393216 | bytes 4718592 | tf_op jit(solution)/shard_map/add | solution.py:57
  98.5 17.9 %all-to-all-done.2 = f32[3,8,32,512]{3,2,0,1:T(8,128)S(1)} async-done(((f32[3,8,32,512]{3,2,0,1:T(8,128)}), f32[3,8,32,512]{3,2,0,1:T(8,128)S(1)}, u32[]{:S(2)}, u32[]{:S(2)}) %all-to-all-start.2) | async-done | bytes 1572896 | tf_op jit(solution)/shard_map/all_to_all | solution.py:117
  116.4 6.2 %all-to-all-start.1 = ((f32[3,8,32,512]{3,2,0,1:T(8,128)}), f32[3,8,32,512]{3,2,0,1:T(8,128)S(1)}, u32[]{:S(2)}, u32[]{:S(2)}) async-start(f32[3,8,32,512]{3,2,0,1:T(8,128)} %bitcast_add_fusion.1), calls=%async_computation.1 | async-start | bytes 3145728 | tf_op jit(solution)/shard_map/all_to_all | solution.py:117
  123.5 5.1 %collective-permute-start.10 = (f32[3,32,1024]{2,1,0:T(8,128)}, f32[3,32,1024]{2,1,0:T(8,128)}, u32[]{:S(2)}, u32[]{:S(2)}) collective-permute-start(f32[3,32,1024]{2,1,0:T(8,128)} %pad_maximum_fusion.2), channel_id=1, source_target_pairs={{0,0},{1,8},{2,16},{3,24},{4,32},{5,40},{6,48},{7,56},{8,1},{9,9},... | collective-permute-start | bytes 1179656 | tf_op jit(solution)/shard_map/ppermute | solution.py:81
  128.8 31.1 %collective-permute-done.10 = f32[3,32,1024]{2,1,0:T(8,128)} collective-permute-done((f32[3,32,1024]{2,1,0:T(8,128)}, f32[3,32,1024]{2,1,0:T(8,128)}, u32[]{:S(2)}, u32[]{:S(2)}) %collective-permute-start.10) | collective-permute-done | bytes 393248 | tf_op jit(solution)/shard_map/ppermute | solution.py:81
  160.0 2.0 convolution_bitcast_fusion
  162.2 2.0 convolution_bitcast_fusion.1
  166.9 1.7 collective-permute-done.11
  169.2 20.7 %all_to_all.33 = f32[64,1,2560]{2,1,0:T(1,128)S(1)} all-to-all(f32[64,1,2560]{2,1,0:T(1,128)S(1)} %all_to_all.24), channel_id=1, replica_groups=mesh['prow_hi'=8,'core'=2,'pcol'=8] {'prow_hi','pcol'}, dimensions={0} | all-to-all | bytes 1310720 | tf_op jit(solution)/shard_map/all_to_all | solution.py:159
  190.6 18.4 %all_to_all.34 = f32[64,1,2560]{2,1,0:T(1,128)S(1)} all-to-all(f32[64,1,2560]{2,1,0:T(1,128)S(1)} %broadcast_in_dim.43), channel_id=1, replica_groups=mesh['prow_hi'=8,'core'=2,'pcol'=8] {'prow_hi','pcol'}, dimensions={0} | all-to-all | bytes 1310720 | tf_op jit(solution)/shard_map/all_to_all | solution.py:161
  209.9 5.1 %collective-permute-start.9 = (f32[3,32,1024]{2,1,0:T(8,128)}, f32[3,32,1024]{2,1,0:T(8,128)S(1)}, u32[]{:S(2)}, u32[]{:S(2)}) collective-permute-start(f32[3,32,1024]{2,1,0:T(8,128)} %pad_maximum_fusion.1), channel_id=1, source_target_pairs={{0,0},{8,1},{16,2},{24,3},{32,4},{40,5},{48,6},{56,7},{1,8},{9,9},... | collective-permute-start | bytes 1179656 | tf_op jit(solution)/shard_map/ppermute | solution.py:153
  215.0 19.6 %collective-permute-done.9 = f32[3,32,1024]{2,1,0:T(8,128)S(1)} collective-permute-done((f32[3,32,1024]{2,1,0:T(8,128)}, f32[3,32,1024]{2,1,0:T(8,128)S(1)}, u32[]{:S(2)}, u32[]{:S(2)}) %collective-permute-start.9) | collective-permute-done | bytes 393248 | tf_op jit(solution)/shard_map/ppermute | solution.py:153
  235.8 1.9 maximum_select_fusion
  241.4 1.8 fusion.8
  (95 shorter events, 34.9 us)
Async XLA Ops:
  3.4 18.8 %collective-permute-start.1 = (f32[3,32,512]{2,1,0:T(8,128)S(1)}, f32[3,32,512]{2,1,0:T(8,128)S(1)}, u32[]{:S(2)}, u32[]{:S(2)}) collective-permute-start(f32[3,32,512]{2,1,0:T(8,128)S(1)} %bitcast_multiply_fusion.1), channel_id=1, source_target_pairs={{0,1},{1,2},{2,3},{3,4},{4,5},{5,6},{6,7},{7,0},{8,9},{9,10},{10,1... | collective-permute-start | bytes 589832 | tf_op jit(solution)/shard_map/ppermute | solution.py:94
  5.4 20.5 %collective-permute-start.2 = (f32[3,32,512]{2,1,0:T(8,128)S(1)}, f32[3,32,512]{2,1,0:T(8,128)S(1)}, u32[]{:S(2)}, u32[]{:S(2)}) collective-permute-start(f32[3,32,512]{2,1,0:T(8,128)S(1)} %bitcast_multiply_fusion.1), channel_id=1, source_target_pairs={{0,2},{1,3},{2,4},{3,5},{4,6},{5,7},{6,0},{7,1},{8,10},{9,11},{10,... | collective-permute-start | bytes 589832 | tf_op jit(solution)/shard_map/ppermute | solution.py:94
  8.9 18.8 %collective-permute-start.3 = (f32[3,32,512]{2,1,0:T(8,128)S(1)}, f32[3,32,512]{2,1,0:T(8,128)S(1)}, u32[]{:S(2)}, u32[]{:S(2)}) collective-permute-start(f32[3,32,512]{2,1,0:T(8,128)S(1)} %bitcast_multiply_fusion.1), channel_id=1, source_target_pairs={{0,3},{1,4},{2,5},{3,6},{4,7},{5,0},{6,1},{7,2},{8,11},{9,12},{10,... | collective-permute-start | bytes 589832 | tf_op jit(solution)/shard_map/ppermute | solution.py:94
  10.2 18.3 %collective-permute-start.4 = (f32[3,32,512]{2,1,0:T(8,128)S(1)}, f32[3,32,512]{2,1,0:T(8,128)S(1)}, u32[]{:S(2)}, u32[]{:S(2)}) collective-permute-start(f32[3,32,512]{2,1,0:T(8,128)S(1)} %bitcast_multiply_fusion.1), channel_id=1, source_target_pairs={{0,4},{1,5},{2,6},{3,7},{4,0},{5,1},{6,2},{7,3},{8,12},{9,13},{10,... | collective-permute-start | bytes 589832 | tf_op jit(solution)/shard_map/ppermute | solution.py:94
  11.4 17.8 %collective-permute-start.5 = (f32[3,32,512]{2,1,0:T(8,128)S(1)}, f32[3,32,512]{2,1,0:T(8,128)S(1)}, u32[]{:S(2)}, u32[]{:S(2)}) collective-permute-start(f32[3,32,512]{2,1,0:T(8,128)S(1)} %bitcast_multiply_fusion.1), channel_id=1, source_target_pairs={{0,5},{1,6},{2,7},{3,0},{4,1},{5,2},{6,3},{7,4},{8,13},{9,14},{10,... | collective-permute-start | bytes 589832 | tf_op jit(solution)/shard_map/ppermute | solution.py:94
  15.5 4.9 %copy-start.3 = (f32[3,1,32,512]{3,2,1,0:T(8,128)S(1)}, f32[3,1,32,512]{3,2,1,0:T(8,128)}, u32[]{:S(2)}) copy-start(f32[3,1,32,512]{3,2,1,0:T(8,128)} %param.9) | copy-start | bytes 589828
  15.5 57.0 %all-to-all-start = ((f32[3,256,512]{2,0,1:T(4,128)}), f32[3,256,512]{2,0,1:T(4,128)S(1)}, u32[]{:S(2)}, u32[]{:S(2)}) async-start(f32[3,256,512]{2,0,1:T(4,128)} %bitcast.1), calls=%async_computation | async-start | bytes 4194304 | tf_op jit(solution)/shard_map/all_to_all | solution.py:105
  22.2 31.3 %collective-permute-start.6 = (f32[3,32,512]{2,1,0:T(8,128)S(1)}, f32[3,32,512]{2,1,0:T(8,128)S(1)}, u32[]{:S(2)}, u32[]{:S(2)}) collective-permute-start(f32[3,32,512]{2,1,0:T(8,128)S(1)} %bitcast_multiply_fusion.1), channel_id=1, source_target_pairs={{0,6},{1,7},{2,0},{3,1},{4,2},{5,3},{6,4},{7,5},{8,14},{9,15},{10,... | collective-permute-start | bytes 589832 | tf_op jit(solution)/shard_map/ppermute | solution.py:94
  25.9 28.3 %collective-permute-start.7 = (f32[3,32,512]{2,1,0:T(8,128)S(1)}, f32[3,32,512]{2,1,0:T(8,128)S(1)}, u32[]{:S(2)}, u32[]{:S(2)}) collective-permute-start(f32[3,32,512]{2,1,0:T(8,128)S(1)} %bitcast_multiply_fusion.1), channel_id=1, source_target_pairs={{0,7},{1,0},{2,1},{3,2},{4,3},{5,4},{6,5},{7,6},{8,15},{9,8},{10,9... | collective-permute-start | bytes 589832 | tf_op jit(solution)/shard_map/ppermute | solution.py:94
  72.5 12.6 %collective-permute-start.8 = (f32[3,8,32,512]{3,2,0,1:T(8,128)}, f32[3,8,32,512]{3,2,0,1:T(8,128)}, u32[]{:S(2)}, u32[]{:S(2)}) collective-permute-start(f32[3,8,32,512]{3,2,0,1:T(8,128)} %bitcast.180), channel_id=1, source_target_pairs={{0,8},{8,0},{1,9},{9,1},{2,10},{10,2},{3,11},{11,3},{4,12},{12,4},... | collective-permute-start | bytes 4718600 | tf_op jit(solution)/shard_map/ppermute | solution.py:57
  83.2 2.0 copy-start
  84.6 11.0 %collective-permute-start = (f32[3,8,32,512]{3,2,0,1:T(8,128)}, f32[3,8,32,512]{3,2,0,1:T(8,128)}, u32[]{:S(2)}, u32[]{:S(2)}) collective-permute-start(f32[3,8,32,512]{3,2,0,1:T(8,128)} %bitcast.181), channel_id=1, source_target_pairs={{0,8},{8,0},{1,9},{9,1},{2,10},{10,2},{3,11},{11,3},{4,12},{12,4},... | collective-permute-start | bytes 4718600 | tf_op jit(solution)/shard_map/ppermute | solution.py:57
  88.2 28.2 %all-to-all-start.2 = ((f32[3,8,32,512]{3,2,0,1:T(8,128)}), f32[3,8,32,512]{3,2,0,1:T(8,128)S(1)}, u32[]{:S(2)}, u32[]{:S(2)}) async-start(f32[3,8,32,512]{3,2,0,1:T(8,128)} %bitcast_add_fusion), calls=%async_computation.2 | async-start | bytes 3145728 | tf_op jit(solution)/shard_map/all_to_all | solution.py:117
  98.5 24.1 %copy-start.4 = (f32[3,1,32,512]{3,2,1,0:T(8,128)S(1)}, f32[3,1,32,512]{3,2,1,0:T(8,128)}, u32[]{:S(2)}) copy-start(f32[3,1,32,512]{3,2,1,0:T(8,128)} %param.8) | copy-start | bytes 589828
  116.4 45.5 %all-to-all-start.1 = ((f32[3,8,32,512]{3,2,0,1:T(8,128)}), f32[3,8,32,512]{3,2,0,1:T(8,128)S(1)}, u32[]{:S(2)}, u32[]{:S(2)}) async-start(f32[3,8,32,512]{3,2,0,1:T(8,128)} %bitcast_add_fusion.1), calls=%async_computation.1 | async-start | bytes 3145728 | tf_op jit(solution)/shard_map/all_to_all | solution.py:117
  123.5 36.5 %collective-permute-start.10 = (f32[3,32,1024]{2,1,0:T(8,128)}, f32[3,32,1024]{2,1,0:T(8,128)}, u32[]{:S(2)}, u32[]{:S(2)}) collective-permute-start(f32[3,32,1024]{2,1,0:T(8,128)} %pad_maximum_fusion.2), channel_id=1, source_target_pairs={{0,0},{1,8},{2,16},{3,24},{4,32},{5,40},{6,48},{7,56},{8,1},{9,9},... | collective-permute-start | bytes 1179656 | tf_op jit(solution)/shard_map/ppermute | solution.py:81
  166.4 2.2 collective-permute-start.11
  209.0 26.4 %collective-permute-start.12 = (f32[64,2560]{1,0:T(8,128)S(1)}, f32[64,2560]{1,0:T(8,128)S(1)}, u32[]{:S(2)}, u32[]{:S(2)}) collective-permute-start(f32[64,2560]{1,0:T(8,128)S(1)} %bitcast.191), channel_id=1, source_target_pairs={{0,8},{8,0},{1,9},{9,1},{2,10},{10,2},{3,11},{11,3},{4,12},{12,4},... | collective-permute-start | bytes 1966088 | tf_op jit(solution)/shard_map/ppermute | solution.py:162
  209.9 24.7 %collective-permute-start.9 = (f32[3,32,1024]{2,1,0:T(8,128)}, f32[3,32,1024]{2,1,0:T(8,128)S(1)}, u32[]{:S(2)}, u32[]{:S(2)}) collective-permute-start(f32[3,32,1024]{2,1,0:T(8,128)} %pad_maximum_fusion.1), channel_id=1, source_target_pairs={{0,0},{8,1},{16,2},{24,3},{32,4},{40,5},{48,6},{56,7},{1,8},{9,9},... | collective-permute-start | bytes 1179656 | tf_op jit(solution)/shard_map/ppermute | solution.py:153
  239.9 1.2 copy-start.1
  239.9 1.5 copy-start.2
where the time goes:
time: 245 us; the launch traced here: 243 us
  waiting for transfers between devices  94 us (38%)
  starting transfers between devices  43.3 us (18%)
  blocking collectives  39.1 us (16%)
  matrix products  24.1 us (10%)
  local copies, waits for them, and re-layouts  23.4 us (10%)
  other arithmetic  18.2 us (7%)
    ppermute x1, waiting for transfers between devices, body(): x_at_reducer = lax.ppermute(x, both, to_reducer)  31.1 us
    ppermute x7, waiting for transfers between devices, gather_piece(): lax.ppermute(piece, 'pcol', [(i, (i + k) % col_count) for i in range(col_...  23.6 us
    all_to_all x1, blocking collectives, body(): reduced = jnp.sum(lax.all_to_all(flat, others, 0, 0, tiled=True), axis=0)  20.7 us
    dot_general x2, matrix products, reduce_gathered(): jnp.einsum('lsmt,lsw->mtw', matrix, gathered, precision=highest, preferre...  20.2 us
    ppermute x1, waiting for transfers between devices, body(): column_home = lax.ppermute(column, both, to_owner)  19.6 us
    all_to_all x1, blocking collectives, body(): lax.all_to_all(spread_sum, others, 0, 0, tiled=True).reshape(half.shape)  18.4 us
    all_to_all x2, waiting for transfers between devices, reduce_gathered(): received = lax.all_to_all(pair_sum(chunks, 1), 'prow_hi', 1, 1, tiled=True)  17.9 us
    all_to_all x2, starting transfers between devices, reduce_gathered(): received = lax.all_to_all(pair_sum(chunks, 1), 'prow_hi', 1, 1, tiled=True)  13.6 us
  transfers between devices with their start and end apart: 16, of which 5 were waited for; matrix products, arithmetic and copies ran while one was open for 20% of the time, Pallas kernels for 0%

commit v1 on v0

--- a/solution.py
+++ b/solution.py
@@ -106,19 +106,26 @@
         return gathered
 
     def reduce_gathered(piece, gathered):
-        partial = jnp.einsum(
+        partial = product_of(gathered)
+        chunks = partial.reshape(row_blocks, row_count, slice_rows, piece.shape[-1])
+        pre = pair_sum(chunks, 1)
+        received = lax.all_to_all(pre, "prow_hi", 1, 1, tiled=True)
+        return jnp.sum(received, axis=1)
+
+    def product_of(gathered):
+        return jnp.einsum(
             "lsmt,lsw->mtw",
             matrix,
             gathered,
             precision=highest,
             preferred_element_type=jnp.float32,
         )
-        chunks = partial.reshape(row_blocks, row_count, slice_rows, piece.shape[-1])
-        received = lax.all_to_all(pair_sum(chunks, 1), "prow_hi", 1, 1, tiled=True)
-        return jnp.sum(received, axis=1)
 
     total = jnp.concatenate(
-        [reduce_inner(x[..., k * PIECE:(k + 1) * PIECE], k > 0) for k in range(2 * width // PIECE)],
+        [
+            reduce_inner(x[..., k * PIECE:(k + 1) * PIECE], k > 0)
+            for k in range(2 * width // PIECE)
+        ],
         axis=-1,
     )
 

time: 245 us -> 245 us (level)
  no operation moved by 1% of the time
where the time goes in v1:
time: 245 us; the launch traced here: 243 us
  waiting for transfers between devices  94 us (38%)
  starting transfers between devices  43.3 us (18%)
  blocking collectives  39.1 us (16%)
  matrix products  24.1 us (10%)
  local copies, waits for them, and re-layouts  23.4 us (10%)
  other arithmetic  18.2 us (7%)
    ppermute x1, waiting for transfers between devices, body(): x_at_reducer = lax.ppermute(x, both, to_reducer)  31.1 us
    ppermute x7, waiting for transfers between devices, gather_piece(): lax.ppermute(piece, 'pcol', [(i, (i + k) % col_count) for i in range(col_...  23.6 us
    all_to_all x1, blocking collectives, body(): reduced = jnp.sum(lax.all_to_all(flat, others, 0, 0, tiled=True), axis=0)  20.7 us
    dot_general x2, matrix products, product_of(): jnp.einsum('lsmt,lsw->mtw', matrix, gathered, precision=highest, preferre...  20.2 us
    ppermute x1, waiting for transfers between devices, body(): column_home = lax.ppermute(column, both, to_owner)  19.6 us
    all_to_all x1, blocking collectives, body(): lax.all_to_all(spread_sum, others, 0, 0, tiled=True).reshape(half.shape)  18.4 us
    all_to_all x2, waiting for transfers between devices, reduce_gathered(): received = lax.all_to_all(pre, 'prow_hi', 1, 1, tiled=True)  17.9 us
    all_to_all x2, starting transfers between devices, reduce_gathered(): received = lax.all_to_all(pre, 'prow_hi', 1, 1, tiled=True)  13.6 us
  transfers between devices with their start and end apart: 16, of which 5 were waited for; matrix products, arithmetic and copies ran while one was open for 20% of the time, Pallas kernels for 0%

profile of v1, /device:TPU:6, one launch (start us, length us, event | category | flops | bytes accessed | tf_op | source)
XLA Modules:
  0.0 243.2 jit_solution(8881438911809171003)
XLA Ops:
  3.4 2.0 collective-permute-start.1
  5.4 3.6 %collective-permute-start.2 = (f32[3,32,512]{2,1,0:T(8,128)S(1)}, f32[3,32,512]{2,1,0:T(8,128)S(1)}, u32[]{:S(2)}, u32[]{:S(2)}) collective-permute-start(f32[3,32,512]{2,1,0:T(8,128)S(1)} %bitcast_multiply_fusion.1), channel_id=1, source_target_pairs={{0,2},{1,3},{2,4},{3,5},{4,6},{5,7},{6,0},{7,1},{8,10},{9,11},{10,... | collective-permute-start | bytes 589832 | tf_op jit(solution)/shard_map/ppermute | solution.py:94
  15.5 4.9 %all-to-all-start = ((f32[3,256,512]{2,0,1:T(4,128)}), f32[3,256,512]{2,0,1:T(4,128)S(1)}, u32[]{:S(2)}, u32[]{:S(2)}) async-start(f32[3,256,512]{2,0,1:T(4,128)} %bitcast.1), calls=%async_computation | async-start | bytes 4194304 | tf_op jit(solution)/shard_map/all_to_all | solution.py:105
  22.2 3.0 %collective-permute-start.6 = (f32[3,32,512]{2,1,0:T(8,128)S(1)}, f32[3,32,512]{2,1,0:T(8,128)S(1)}, u32[]{:S(2)}, u32[]{:S(2)}) collective-permute-start(f32[3,32,512]{2,1,0:T(8,128)S(1)} %bitcast_multiply_fusion.1), channel_id=1, source_target_pairs={{0,6},{1,7},{2,0},{3,1},{4,2},{5,3},{6,4},{7,5},{8,14},{9,15},{10,... | collective-permute-start | bytes 589832 | tf_op jit(solution)/shard_map/ppermute | solution.py:94
  29.9 23.6 %collective-permute-done.6 = f32[3,32,512]{2,1,0:T(8,128)S(1)} collective-permute-done((f32[3,32,512]{2,1,0:T(8,128)S(1)}, f32[3,32,512]{2,1,0:T(8,128)S(1)}, u32[]{:S(2)}, u32[]{:S(2)}) %collective-permute-start.6) | collective-permute-done | bytes 196640 | tf_op jit(solution)/shard_map/ppermute | solution.py:94
  54.9 3.2 %gather_fusion = f32[8,3,32,512]{3,2,1,0:T(8,128)} fusion(f32[3,8,32,512]{3,2,0,1:T(8,128)} %bitcast_dynamic-update-slice_fusion, s32[1024]{0:T(1024)S(1)} %pad_clamp_fusion), kind=kCustom, calls=%fused_computation | custom fusion | bytes 3145760 | tf_op jit(solution)/shard_map/jit(_take)/gather | solution.py:100
  59.9 9.8 %fusion = f32[512,6,256,1]{0,2,3,1:T(8,128)S(1)} fusion(f32[3,256,512,1]{2,1,0,3:T(8,128)S(1)} %bitcast.186, f32[3,1,256,6,1,256]{5,4,3,2,1,0:T(1,128)} %param.7), kind=kOutput, calls=%fused_computation.1 | convolution fusion | flops 7247757312 | bytes 9437184 | tf_op jit(solution)/shard_map/lsmt,lsw->mtw/dot_general | solution.py:116
  72.5 10.4 %fusion.2 = f32[512,6,256,1]{0,2,3,1:T(8,128)S(1)} fusion(f32[3,1,256,6,1,256]{5,4,3,2,1,0:T(1,128)} %param.7, f32[3,256,512]{2,0,1:T(4,128)S(1)} %all-to-all-done), kind=kOutput, calls=%fused_computation.3 | convolution fusion | flops 7247757312 | bytes 9437184 | tf_op jit(solution)/shard_map/lsmt,lsw->mtw/dot_general | solution.py:116
  85.2 2.9 %bitcast_add_fusion = f32[3,8,32,512]{3,2,0,1:T(8,128)} fusion(f32[3,8,32,512]{3,2,0,1:T(8,128)} %collective-permute-done.8, f32[3,8,1,32,512]{4,3,2,1,0:T(8,128)S(1)} %copy-done), kind=kLoop, calls=%fused_computation.8 | loop fusion | flops 393216 | bytes 4718592 | tf_op jit(solution)/shard_map/add | solution.py:57
  88.2 7.4 %all-to-all-start.2 = ((f32[3,8,32,512]{3,2,0,1:T(8,128)}), f32[3,8,32,512]{3,2,0,1:T(8,128)S(1)}, u32[]{:S(2)}, u32[]{:S(2)}) async-start(f32[3,8,32,512]{3,2,0,1:T(8,128)} %bitcast_add_fusion), calls=%async_computation.2 | async-start | bytes 3145728 | tf_op jit(solution)/shard_map/all_to_all | solution.py:112
  95.6 2.9 %bitcast_add_fusion.1 = f32[3,8,32,512]{3,2,0,1:T(8,128)} fusion(f32[3,8,32,512]{3,2,0,1:T(8,128)} %collective-permute-done, f32[3,8,1,32,512]{4,3,2,1,0:T(8,128)S(1)} %get-tuple-element.10), kind=kLoop, calls=%fused_computation.9 | loop fusion | flops 393216 | bytes 4718592 | tf_op jit(solution)/shard_map/add | solution.py:57
  98.5 17.9 %all-to-all-done.2 = f32[3,8,32,512]{3,2,0,1:T(8,128)S(1)} async-done(((f32[3,8,32,512]{3,2,0,1:T(8,128)}), f32[3,8,32,512]{3,2,0,1:T(8,128)S(1)}, u32[]{:S(2)}, u32[]{:S(2)}) %all-to-all-start.2) | async-done | bytes 1572896 | tf_op jit(solution)/shard_map/all_to_all | solution.py:112
  116.4 6.2 %all-to-all-start.1 = ((f32[3,8,32,512]{3,2,0,1:T(8,128)}), f32[3,8,32,512]{3,2,0,1:T(8,128)S(1)}, u32[]{:S(2)}, u32[]{:S(2)}) async-start(f32[3,8,32,512]{3,2,0,1:T(8,128)} %bitcast_add_fusion.1), calls=%async_computation.1 | async-start | bytes 3145728 | tf_op jit(solution)/shard_map/all_to_all | solution.py:112
  123.5 5.1 %collective-permute-start.10 = (f32[3,32,1024]{2,1,0:T(8,128)}, f32[3,32,1024]{2,1,0:T(8,128)}, u32[]{:S(2)}, u32[]{:S(2)}) collective-permute-start(f32[3,32,1024]{2,1,0:T(8,128)} %pad_maximum_fusion.2), channel_id=1, source_target_pairs={{0,0},{1,8},{2,16},{3,24},{4,32},{5,40},{6,48},{7,56},{8,1},{9,9},... | collective-permute-start | bytes 1179656 | tf_op jit(solution)/shard_map/ppermute | solution.py:81
  128.8 31.1 %collective-permute-done.10 = f32[3,32,1024]{2,1,0:T(8,128)} collective-permute-done((f32[3,32,1024]{2,1,0:T(8,128)}, f32[3,32,1024]{2,1,0:T(8,128)}, u32[]{:S(2)}, u32[]{:S(2)}) %collective-permute-start.10) | collective-permute-done | bytes 393248 | tf_op jit(solution)/shard_map/ppermute | solution.py:81
  160.0 2.0 convolution_bitcast_fusion
  162.2 2.0 convolution_bitcast_fusion.1
  166.9 1.7 collective-permute-done.11
  169.2 20.7 %all_to_all.33 = f32[64,1,2560]{2,1,0:T(1,128)S(1)} all-to-all(f32[64,1,2560]{2,1,0:T(1,128)S(1)} %all_to_all.24), channel_id=1, replica_groups=mesh['prow_hi'=8,'core'=2,'pcol'=8] {'prow_hi','pcol'}, dimensions={0} | all-to-all | bytes 1310720 | tf_op jit(solution)/shard_map/all_to_all | solution.py:166
  190.6 18.4 %all_to_all.34 = f32[64,1,2560]{2,1,0:T(1,128)S(1)} all-to-all(f32[64,1,2560]{2,1,0:T(1,128)S(1)} %broadcast_in_dim.43), channel_id=1, replica_groups=mesh['prow_hi'=8,'core'=2,'pcol'=8] {'prow_hi','pcol'}, dimensions={0} | all-to-all | bytes 1310720 | tf_op jit(solution)/shard_map/all_to_all | solution.py:168
  209.9 5.1 %collective-permute-start.9 = (f32[3,32,1024]{2,1,0:T(8,128)}, f32[3,32,1024]{2,1,0:T(8,128)S(1)}, u32[]{:S(2)}, u32[]{:S(2)}) collective-permute-start(f32[3,32,1024]{2,1,0:T(8,128)} %pad_maximum_fusion.1), channel_id=1, source_target_pairs={{0,0},{8,1},{16,2},{24,3},{32,4},{40,5},{48,6},{56,7},{1,8},{9,9},... | collective-permute-start | bytes 1179656 | tf_op jit(solution)/shard_map/ppermute | solution.py:160
  215.0 19.6 %collective-permute-done.9 = f32[3,32,1024]{2,1,0:T(8,128)S(1)} collective-permute-done((f32[3,32,1024]{2,1,0:T(8,128)}, f32[3,32,1024]{2,1,0:T(8,128)S(1)}, u32[]{:S(2)}, u32[]{:S(2)}) %collective-permute-start.9) | collective-permute-done | bytes 393248 | tf_op jit(solution)/shard_map/ppermute | solution.py:160
  235.8 1.9 maximum_select_fusion
  241.4 1.8 fusion.8
  (95 shorter events, 34.9 us)
Async XLA Ops:
  3.4 18.8 %collective-permute-start.1 = (f32[3,32,512]{2,1,0:T(8,128)S(1)}, f32[3,32,512]{2,1,0:T(8,128)S(1)}, u32[]{:S(2)}, u32[]{:S(2)}) collective-permute-start(f32[3,32,512]{2,1,0:T(8,128)S(1)} %bitcast_multiply_fusion.1), channel_id=1, source_target_pairs={{0,1},{1,2},{2,3},{3,4},{4,5},{5,6},{6,7},{7,0},{8,9},{9,10},{10,1... | collective-permute-start | bytes 589832 | tf_op jit(solution)/shard_map/ppermute | solution.py:94
  5.4 20.5 %collective-permute-start.2 = (f32[3,32,512]{2,1,0:T(8,128)S(1)}, f32[3,32,512]{2,1,0:T(8,128)S(1)}, u32[]{:S(2)}, u32[]{:S(2)}) collective-permute-start(f32[3,32,512]{2,1,0:T(8,128)S(1)} %bitcast_multiply_fusion.1), channel_id=1, source_target_pairs={{0,2},{1,3},{2,4},{3,5},{4,6},{5,7},{6,0},{7,1},{8,10},{9,11},{10,... | collective-permute-start | bytes 589832 | tf_op jit(solution)/shard_map/ppermute | solution.py:94
  8.9 18.8 %collective-permute-start.3 = (f32[3,32,512]{2,1,0:T(8,128)S(1)}, f32[3,32,512]{2,1,0:T(8,128)S(1)}, u32[]{:S(2)}, u32[]{:S(2)}) collective-permute-start(f32[3,32,512]{2,1,0:T(8,128)S(1)} %bitcast_multiply_fusion.1), channel_id=1, source_target_pairs={{0,3},{1,4},{2,5},{3,6},{4,7},{5,0},{6,1},{7,2},{8,11},{9,12},{10,... | collective-permute-start | bytes 589832 | tf_op jit(solution)/shard_map/ppermute | solution.py:94
  10.2 18.3 %collective-permute-start.4 = (f32[3,32,512]{2,1,0:T(8,128)S(1)}, f32[3,32,512]{2,1,0:T(8,128)S(1)}, u32[]{:S(2)}, u32[]{:S(2)}) collective-permute-start(f32[3,32,512]{2,1,0:T(8,128)S(1)} %bitcast_multiply_fusion.1), channel_id=1, source_target_pairs={{0,4},{1,5},{2,6},{3,7},{4,0},{5,1},{6,2},{7,3},{8,12},{9,13},{10,... | collective-permute-start | bytes 589832 | tf_op jit(solution)/shard_map/ppermute | solution.py:94
  11.4 17.8 %collective-permute-start.5 = (f32[3,32,512]{2,1,0:T(8,128)S(1)}, f32[3,32,512]{2,1,0:T(8,128)S(1)}, u32[]{:S(2)}, u32[]{:S(2)}) collective-permute-start(f32[3,32,512]{2,1,0:T(8,128)S(1)} %bitcast_multiply_fusion.1), channel_id=1, source_target_pairs={{0,5},{1,6},{2,7},{3,0},{4,1},{5,2},{6,3},{7,4},{8,13},{9,14},{10,... | collective-permute-start | bytes 589832 | tf_op jit(solution)/shard_map/ppermute | solution.py:94
  15.5 4.9 %copy-start.3 = (f32[3,1,32,512]{3,2,1,0:T(8,128)S(1)}, f32[3,1,32,512]{3,2,1,0:T(8,128)}, u32[]{:S(2)}) copy-start(f32[3,1,32,512]{3,2,1,0:T(8,128)} %param.9) | copy-start | bytes 589828
  15.5 57.0 %all-to-all-start = ((f32[3,256,512]{2,0,1:T(4,128)}), f32[3,256,512]{2,0,1:T(4,128)S(1)}, u32[]{:S(2)}, u32[]{:S(2)}) async-start(f32[3,256,512]{2,0,1:T(4,128)} %bitcast.1), calls=%async_computation | async-start | bytes 4194304 | tf_op jit(solution)/shard_map/all_to_all | solution.py:105
  22.2 31.3 %collective-permute-start.6 = (f32[3,32,512]{2,1,0:T(8,128)S(1)}, f32[3,32,512]{2,1,0:T(8,128)S(1)}, u32[]{:S(2)}, u32[]{:S(2)}) collective-permute-start(f32[3,32,512]{2,1,0:T(8,128)S(1)} %bitcast_multiply_fusion.1), channel_id=1, source_target_pairs={{0,6},{1,7},{2,0},{3,1},{4,2},{5,3},{6,4},{7,5},{8,14},{9,15},{10,... | collective-permute-start | bytes 589832 | tf_op jit(solution)/shard_map/ppermute | solution.py:94
  25.9 28.3 %collective-permute-start.7 = (f32[3,32,512]{2,1,0:T(8,128)S(1)}, f32[3,32,512]{2,1,0:T(8,128)S(1)}, u32[]{:S(2)}, u32[]{:S(2)}) collective-permute-start(f32[3,32,512]{2,1,0:T(8,128)S(1)} %bitcast_multiply_fusion.1), channel_id=1, source_target_pairs={{0,7},{1,0},{2,1},{3,2},{4,3},{5,4},{6,5},{7,6},{8,15},{9,8},{10,9... | collective-permute-start | bytes 589832 | tf_op jit(solution)/shard_map/ppermute | solution.py:94
  72.5 12.6 %collective-permute-start.8 = (f32[3,8,32,512]{3,2,0,1:T(8,128)}, f32[3,8,32,512]{3,2,0,1:T(8,128)}, u32[]{:S(2)}, u32[]{:S(2)}) collective-permute-start(f32[3,8,32,512]{3,2,0,1:T(8,128)} %bitcast.180), channel_id=1, source_target_pairs={{0,8},{8,0},{1,9},{9,1},{2,10},{10,2},{3,11},{11,3},{4,12},{12,4},... | collective-permute-start | bytes 4718600 | tf_op jit(solution)/shard_map/ppermute | solution.py:57
  83.2 2.0 copy-start
  84.6 11.0 %collective-permute-start = (f32[3,8,32,512]{3,2,0,1:T(8,128)}, f32[3,8,32,512]{3,2,0,1:T(8,128)}, u32[]{:S(2)}, u32[]{:S(2)}) collective-permute-start(f32[3,8,32,512]{3,2,0,1:T(8,128)} %bitcast.181), channel_id=1, source_target_pairs={{0,8},{8,0},{1,9},{9,1},{2,10},{10,2},{3,11},{11,3},{4,12},{12,4},... | collective-permute-start | bytes 4718600 | tf_op jit(solution)/shard_map/ppermute | solution.py:57
  88.2 28.2 %all-to-all-start.2 = ((f32[3,8,32,512]{3,2,0,1:T(8,128)}), f32[3,8,32,512]{3,2,0,1:T(8,128)S(1)}, u32[]{:S(2)}, u32[]{:S(2)}) async-start(f32[3,8,32,512]{3,2,0,1:T(8,128)} %bitcast_add_fusion), calls=%async_computation.2 | async-start | bytes 3145728 | tf_op jit(solution)/shard_map/all_to_all | solution.py:112
  98.5 24.1 %copy-start.4 = (f32[3,1,32,512]{3,2,1,0:T(8,128)S(1)}, f32[3,1,32,512]{3,2,1,0:T(8,128)}, u32[]{:S(2)}) copy-start(f32[3,1,32,512]{3,2,1,0:T(8,128)} %param.8) | copy-start | bytes 589828
  116.4 45.5 %all-to-all-start.1 = ((f32[3,8,32,512]{3,2,0,1:T(8,128)}), f32[3,8,32,512]{3,2,0,1:T(8,128)S(1)}, u32[]{:S(2)}, u32[]{:S(2)}) async-start(f32[3,8,32,512]{3,2,0,1:T(8,128)} %bitcast_add_fusion.1), calls=%async_computation.1 | async-start | bytes 3145728 | tf_op jit(solution)/shard_map/all_to_all | solution.py:112
  123.5 36.5 %collective-permute-start.10 = (f32[3,32,1024]{2,1,0:T(8,128)}, f32[3,32,1024]{2,1,0:T(8,128)}, u32[]{:S(2)}, u32[]{:S(2)}) collective-permute-start(f32[3,32,1024]{2,1,0:T(8,128)} %pad_maximum_fusion.2), channel_id=1, source_target_pairs={{0,0},{1,8},{2,16},{3,24},{4,32},{5,40},{6,48},{7,56},{8,1},{9,9},... | collective-permute-start | bytes 1179656 | tf_op jit(solution)/shard_map/ppermute | solution.py:81
  166.4 2.2 collective-permute-start.11
  209.0 26.4 %collective-permute-start.12 = (f32[64,2560]{1,0:T(8,128)S(1)}, f32[64,2560]{1,0:T(8,128)S(1)}, u32[]{:S(2)}, u32[]{:S(2)}) collective-permute-start(f32[64,2560]{1,0:T(8,128)S(1)} %bitcast.191), channel_id=1, source_target_pairs={{0,8},{8,0},{1,9},{9,1},{2,10},{10,2},{3,11},{11,3},{4,12},{12,4},... | collective-permute-start | bytes 1966088 | tf_op jit(solution)/shard_map/ppermute | solution.py:169
  209.9 24.7 %collective-permute-start.9 = (f32[3,32,1024]{2,1,0:T(8,128)}, f32[3,32,1024]{2,1,0:T(8,128)S(1)}, u32[]{:S(2)}, u32[]{:S(2)}) collective-permute-start(f32[3,32,1024]{2,1,0:T(8,128)} %pad_maximum_fusion.1), channel_id=1, source_target_pairs={{0,0},{8,1},{16,2},{24,3},{32,4},{40,5},{48,6},{56,7},{1,8},{9,9},... | collective-permute-start | bytes 1179656 | tf_op jit(solution)/shard_map/ppermute | solution.py:160
  239.9 1.2 copy-start.1
  239.9 1.5 copy-start.2
